TPU v7x, 256 devices: a whole 4x4x8 slice. The times are simulated.
256 devices in a mesh: kv: 8 (over x, core), seq: 32 (over z, y).
Axes of the slice: x: 4, y: 4, z: 8, core: 2. Of those that a mesh axis runs over, the one named last changes fastest.
Arguments:
- hidden_states: bfloat16 [6144, 2048], P('seq')
- attn_gain: float32 [2048], replicated, may hold values from 0.5 to 1.5
- w_q: bfloat16 [2048, 2048], P(None, 'kv')
- w_k: bfloat16 [2048, 512], P(None, 'kv')
- w_v: bfloat16 [2048, 512], P(None, 'kv'), may hold values from -0.125 to 0.125
- w_o: bfloat16 [2048, 2048], P('kv'), may hold values from -0.125 to 0.125
- final_gain: float32 [2048], replicated, may hold values from 0.5 to 1.5
- w_head: bfloat16 [2048, 49408], P(None, ('kv', 'seq'))
- doc_lengths: int32 [26], replicated, may hold values from 1 to 3072, as said below
- target_ids: int32 [6144], replicated, may hold values from 0 to 49154, as said below
- vocab_mask: int32 [49408], P(('kv', 'seq')), may hold values from 0 to 1, as said below
Outputs:
- log_probs: float32 [6144], P('seq')
- entropies: float32 [6144], P('seq')
Inputs may be any that keep to these rules, and one draw needn't show every extreme that they name: `doc_lengths`: they sum to 6144; one is 3072, one more is over 1536, every other is under 64. `target_ids`: each names an entry whose vocab_mask is 1. `vocab_mask`: entries from 49155 on are 0.
All inputs are finite; a program needn't handle non-finite values.
Results may differ from a plain program's by a relative error of at most 0.0045.
Values may be sent and summed in bfloat16 or wider, within the bound.
No kernel may reach another device: no remote copies, remote signals or barrier semaphores. Data moves between devices by JAX's collectives and lax.ppermute only.
A program may use at most 128 MiB of HBM per device.

v0:
```python
import math
import jax
import jax.numpy as jnp
from jax import lax
from jax.sharding import Mesh, PartitionSpec as P

HEAD_DIM = 64
ROPE_THETA = 10000000.0
NORM_EPS = 1e-05
NEG_FILL = -1e30
ATTN_SCALE = 0.015625
RESID_SCALE = 5.0
LOGIT_SCALE = 0.125


def rms_norm(values, gain_vec):
    return (
        values * lax.rsqrt(jnp.mean(values * values, axis=-1, keepdims=True) + NORM_EPS) * gain_vec
    )


def rotate(values, positions):
    half_dim = values.shape[-1] // 2
    inverse = jnp.exp(
        jnp.arange(half_dim, dtype=jnp.float32) * (-2.0 * math.log(ROPE_THETA) / values.shape[-1])
    )
    angles = positions.astype(jnp.float32)[:, None] * inverse[None, :]
    cos_val = jnp.cos(angles)[:, None, :]
    sine_val = jnp.sin(angles)[:, None, :]
    lower_half = values[..., :half_dim]
    upper_half = values[..., half_dim:]
    return jnp.concatenate(
        [
            lower_half * cos_val - upper_half * sine_val,
            upper_half * cos_val + lower_half * sine_val,
        ],
        axis=-1,
    )


def local(
    hidden_states,
    attn_gain,
    w_q,
    w_k,
    w_v,
    w_o,
    final_gain,
    w_head,
    doc_lengths,
    target_ids,
    vocab_mask,
):
    tok_rows = hidden_states.shape[0]
    seq_index = lax.axis_index(("z", "y"))
    kv_local = w_k.shape[1] // HEAD_DIM
    q_local = w_q.shape[1] // HEAD_DIM
    group_size = q_local // kv_local
    key_width = kv_local * HEAD_DIM
    stream = hidden_states.astype(jnp.float32)
    normed_in = rms_norm(stream, attn_gain).astype(jnp.bfloat16)
    queries = jnp.dot(normed_in, w_q, preferred_element_type=jnp.float32)
    key_proj = jnp.dot(normed_in, w_k, preferred_element_type=jnp.float32)
    value_proj = jnp.dot(normed_in, w_v, preferred_element_type=jnp.float32)
    token_pos = seq_index * tok_rows + jnp.arange(tok_rows, dtype=jnp.int32)
    doc_ends = jnp.cumsum(doc_lengths)
    doc_starts = doc_ends - doc_lengths
    doc_start = jnp.max(
        jnp.where(doc_starts[None, :] <= token_pos[:, None], doc_starts[None, :], 0), axis=1
    )
    positions = token_pos - doc_start
    rotated_q = rotate(queries.reshape(tok_rows, q_local, HEAD_DIM), positions).astype(jnp.bfloat16)
    rotated_q = rotated_q.reshape(tok_rows, kv_local, group_size, HEAD_DIM)
    rotated_k = rotate(key_proj.reshape(tok_rows, kv_local, HEAD_DIM), positions).astype(
        jnp.bfloat16
    )
    packed = jnp.concatenate(
        [rotated_k.reshape(tok_rows, key_width), value_proj.astype(jnp.bfloat16)], axis=1
    )
    earliest = doc_start[0]
    latest = token_pos[tok_rows - 1]
    initial = (
        jnp.full((kv_local, group_size, tok_rows), NEG_FILL, jnp.float32),
        jnp.zeros((kv_local, group_size, tok_rows), jnp.float32),
        jnp.zeros((kv_local, group_size, tok_rows, HEAD_DIM), jnp.float32),
    )
    shard_rows = lax.all_gather(packed, ("z", "y"), axis=0, tiled=True)
    offset = jnp.int32(0)
    row_count = shard_rows.shape[0]
    key_pos = jnp.arange(row_count, dtype=jnp.int32)

    def update(current):
        top_score, totals, context_sum = current
        key_rows = shard_rows[:, :key_width].reshape(row_count, kv_local, HEAD_DIM)
        value_rows = shard_rows[:, key_width:].reshape(row_count, kv_local, HEAD_DIM)
        scores = (
            jnp.einsum("tkgd,skd->kgts", rotated_q, key_rows, preferred_element_type=jnp.float32)
            * ATTN_SCALE
        )
        allowed = (key_pos[None, :] >= doc_start[:, None]) & (
            key_pos[None, :] <= token_pos[:, None]
        )
        scores = jnp.where(allowed, scores, NEG_FILL)
        new_top = jnp.maximum(top_score, jnp.max(scores, axis=-1))
        weights = jnp.where(allowed, jnp.exp(scores - new_top[..., None]), 0.0)
        rescale = jnp.exp(top_score - new_top)
        totals = jnp.sum(weights, axis=-1)
        context_sum = jnp.einsum(
            "kgts,skd->kgtd",
            weights.astype(jnp.bfloat16),
            value_rows,
            preferred_element_type=jnp.float32,
        )
        return (new_top, totals, context_sum)

    skip_piece = (offset + row_count <= earliest) | (offset > latest)
    top_score, totals, context_sum = lax.cond(skip_piece, lambda current: current, update, initial)
    context = (
        (context_sum / totals[..., None])
        .transpose(2, 0, 1, 3)
        .reshape(tok_rows, q_local * HEAD_DIM)
        .astype(jnp.bfloat16)
    )
    vocab_local = w_head.shape[1]
    y_count = lax.psum(1, "y")
    z_count = lax.psum(1, "z")
    z_index = lax.axis_index("z")
    y_index = lax.axis_index("y")
    kv_index = lax.axis_index("kv")
    attn_out = lax.psum(jnp.dot(context, w_o, preferred_element_type=jnp.float32), "kv")
    final_in = rms_norm(stream + RESID_SCALE * attn_out, final_gain).astype(jnp.bfloat16)
    head_rows = lax.all_gather(final_in, "y", axis=0, tiled=True)
    group_rows = head_rows.shape[0]
    head_cols = lax.all_gather(w_head, "z", axis=1, tiled=True)
    mask_cols = lax.all_gather(vocab_mask, "z", axis=0, tiled=True)
    live_mask = mask_cols == 1
    shard_ids = (
        kv_index * (z_count * y_count) + jnp.arange(z_count, dtype=jnp.int32) * y_count + y_index
    )
    columns = (
        shard_ids[:, None] * vocab_local + jnp.arange(vocab_local, dtype=jnp.int32)[None, :]
    ).reshape(-1)
    row_ids = lax.dynamic_slice_in_dim(target_ids, z_index * group_rows, group_rows, 0)
    logits = jnp.dot(head_rows, head_cols, preferred_element_type=jnp.float32) * LOGIT_SCALE
    masked = jnp.where(live_mask[None, :], logits, NEG_FILL)
    top_row = jnp.max(masked, axis=1)
    shifted = jnp.where(live_mask[None, :], masked - top_row[:, None], 0.0)
    expw = jnp.where(live_mask[None, :], jnp.exp(shifted), 0.0)
    target = jnp.sum(jnp.where(row_ids[:, None] == columns[None, :], logits, 0.0), axis=1)
    row_stats = jnp.stack([top_row, jnp.sum(expw, axis=1), jnp.sum(expw * shifted, axis=1), target])
    top_all = lax.pmax(row_stats[0], ("kv", "y"))
    rescale = jnp.exp(row_stats[0] - top_all)
    total_all, spread_all, target_all = lax.psum(
        (
            row_stats[1] * rescale,
            rescale * (row_stats[2] + (row_stats[0] - top_all) * row_stats[1]),
            row_stats[3],
        ),
        ("kv", "y"),
    )
    log_prob = target_all - top_all - jnp.log(total_all)
    entropy = jnp.log(total_all) - spread_all / total_all
    log_probs = lax.dynamic_slice_in_dim(log_prob, y_index * tok_rows, tok_rows, 0)
    entropies = lax.dynamic_slice_in_dim(entropy, y_index * tok_rows, tok_rows, 0)
    return (log_probs, entropies)


def solution(mesh):
    kv_size, seq_size = mesh.devices.shape
    z_size = mesh.shape["seq"] // 4 if mesh.shape["seq"] % 4 == 0 else mesh.shape["seq"]
    y_size = seq_size // z_size
    split_mesh = Mesh(mesh.devices.reshape(kv_size, z_size, y_size), ("kv", "z", "y"))
    seq = ("z", "y")
    in_specs = (
        P(seq, None),
        P(),
        P(None, "kv"),
        P(None, "kv"),
        P(None, "kv"),
        P("kv", None),
        P(),
        P(None, ("kv",) + seq),
        P(),
        P(),
        P(("kv",) + seq),
    )
    out_specs = (P(seq), P(seq))
    return jax.shard_map(
        local, mesh=split_mesh, in_specs=in_specs, out_specs=out_specs, check_vma=False
    )
```

profile of v0, /device:TPU:32, one launch (start us, length us, event | category | flops | bytes accessed | tf_op | source)
XLA Modules:
  0.0 449.0 jit_solution(1061210086343181944)
XLA Ops:
  8.1 0.9 copy.22
  10.0 1.4 fusion.16
  11.3 1.6 convolution_bitcast_fusion
  13.0 1.6 convolution_convert_fusion
  14.9 0.7 copy.23
  19.0 75.5 %all-gather.5.cloned.1.call-done = bf16[6144,128]{1,0:T(8,128)(2,1)} async-done(((bf16[192,128]{1,0:T(8,128)(2,1)}), bf16[6144,128]{1,0:T(8,128)(2,1)}) %all-gather.5.cloned.1.call-update) | async-done | bytes 1572880 | tf_op jit(solution)/shard_map/all_gather | solution.py:87
  94.5 21.4 %conditional.1 = (f32[1,4,192]{2,1,0:T(4,128)S(1)}, f32[1,4,192,64]{2,3,1,0:T(8,128)S(1)}) conditional(s32[]{:T(128)} %bitcast.9, (s32[6144]{0:T(1024)S(1)}, s32[6144]{0:T(1024)S(1)}, s32[192]{0:T(256)S(1)}, s32[192]{0:T(256)S(1)}, bf16[6144,128]{1,0:T(8,128)(2,1)}, /*index=5*/bf16[192,1,4,64]{0,3,2,1:T(8,128)(2,1)S(1)}) %tuple.16, () %tuple.17), branch_computations={%region_3.6_spmd, %region_6.7_spmd} | conditional | flops 1272839424 | bytes 66424336 | solution.py:117
  94.5 1.0 compare_and_fusion
  95.5 2.6 copy.25
  98.1 5.0 %fusion = (f32[4,192]{1,0:T(4,128)S(1)}, f32[6144,192,4]{0,1,2:T(8,128)S(1)}) fusion(pred[192,6144]{1,0:T(8,128)(4,1)S(1)} %compare_and_fusion, bf16[192,1,4,64]{0,3,2,1:T(8,128)(2,1)S(1)} %get-tuple-element.16, bf16[6144,128]{0,1:T(8,128)(2,1)} %copy.25), kind=kOutput, calls=%fused_computation.2 | convolution fusion | flops 618134784 | bytes 20941824 | tf_op jit(solution)/shard_map/cond/branch_0_fun/tkgd,skd->kgts/dot_general | solution.py:97
  103.1 6.3 %fusion.7 = f32[1,4,192,64]{2,3,1,0:T(8,128)S(1)} fusion(f32[6144,192,4]{0,1,2:T(8,128)S(1)} %get-tuple-element.42, f32[4,192]{1,0:T(4,128)S(1)} %broadcast_maximum_fusion, pred[192,6144]{1,0:T(8,128)(4,1)S(1)} %compare_and_fusion, bf16[6144,128]{0,1:T(8,128)(2,1)} %copy.25), kind=kOutput, calls=%fused_computation.9 | convolution fusion | flops 627572736 | bytes 21040128 | tf_op jit(solution)/shard_map/cond/branch_0_fun/kgts,skd->kgtd/dot_general | solution.py:108
  109.4 6.5 %fusion.2 = f32[4,192]{1,0:T(4,128)S(1)} fusion(f32[6144,192,4]{0,1,2:T(8,128)S(1)} %get-tuple-element.42, f32[4,192]{1,0:T(4,128)S(1)} %broadcast_maximum_fusion, pred[192,6144]{1,0:T(8,128)(4,1)S(1)} %compare_and_fusion), kind=kLoop, calls=%fused_computation.4 | loop fusion | flops 23592192 | bytes 20060160 | tf_op jit(solution)/shard_map/cond/branch_0_fun/reduce_sum | solution.py:107
  115.9 1.6 fusion.35
  118.4 67.6 %all-reduce.4.cloned.1.call-done = f32[192,2048]{1,0:T(8,128)} async-done(((f32[192,2048]{1,0:T(8,128)}), f32[192,2048]{1,0:T(8,128)}) %all-reduce.4.cloned.1.call-update) | async-done | bytes 1572880 | tf_op jit(solution)/shard_map/psum | solution.py:130
  186.1 1.7 multiply_reduce_fusion.1
  187.8 2.6 multiply_convert_fusion
  191.9 0.8 dynamic_slice.9
  192.9 14.0 %all-reduce = s32[1544]{0:T(1024)S(1)} all-reduce(s32[1544]{0:T(1024)S(1)} %dynamic-update-slice), channel_id=1, replica_groups=mesh['kv'=8,'z'=8,'y'=4] {'z'}, use_global_device_ids=true, to_apply=%add | all-reduce | flops 1544 | bytes 12352
  207.0 7.8 %reshape.284 = bf16[1544,2048]{1,0:T(8,128)(2,1)} reshape(bf16[8,193,2048]{2,1,0:T(8,128)(2,1)} %all-gather.9.cloned.1.call-done) | data formatting | bytes 12648448
  214.8 22.4 %all-gather.7.cloned.1.call-done = bf16[768,2048]{1,0:T(8,128)(2,1)} async-done(((bf16[192,2048]{1,0:T(8,128)(2,1)}), bf16[768,2048]{1,0:T(8,128)(2,1)}) %all-gather.7.cloned.1.call-update) | async-done | bytes 3145744 | tf_op jit(solution)/shard_map/all_gather | solution.py:132
  237.2 9.8 %select_reduce_fusion.1 = (f32[768]{0:T(1024)S(1)}, f32[768,1544]{0,1:T(8,128)}) fusion(pred[1544]{0:T(1024)(128)(4,1)S(1)} %broadcast_compare_fusion, bf16[768,2048]{1,0:T(8,128)(2,1)} %all-gather.7.cloned.1.call-done, bf16[1544,2048]{1,0:T(8,128)(2,1)} %reshape.284), kind=kOutput, calls=%fused_computation.23 | convolution fusion | flops 4860560384 | bytes 14217736 | tf_op jit(solution)/shard_map/dot_general | solution.py:144
  247.0 64.9 %pmax.7 = f32[768]{0:T(1024)S(1)} all-reduce(f32[768]{0:T(1024)S(1)} %get-tuple-element.53), channel_id=1, replica_groups=mesh['kv'=8,'z'=8,'y'=4] {'kv','y'}, use_global_device_ids=true, to_apply=%region_12.13 | all-reduce | flops 768 | bytes 6144 | tf_op jit(solution)/shard_map/pmax | solution.py:151
  311.9 4.5 %multiply_reduce_fusion = (f32[768]{0:T(1024)S(1)}, f32[768]{0:T(1024)S(1)}, f32[768]{0:T(1024)S(1)}) fusion(f32[768,1544]{0,1:T(8,128)} %get-tuple-element.54, f32[768]{0:T(1024)S(1)} %get-tuple-element.53, pred[1544]{0:T(1024)(128)(4,1)S(1)} %broadcast_compare_fusion, s32[1544]{0:T(1024)S(1)} %add.107, s32[768]{0:T(1024)S(1)} %dynamic_slice.9), kind=kLoop, calls=%fused_computation.18 | loop fusion | flops 13041408 | bytes 4766248 | tf_op jit(solution)/shard_map/reduce_sum | solution.py:150
  316.5 123.8 %all-reduce.1 = (f32[768]{0:T(1024)S(1)}, f32[768]{0:T(1024)S(1)}, f32[768]{0:T(1024)S(1)}) all-reduce(f32[768]{0:T(1024)S(1)} %get-tuple-element.37, f32[768]{0:T(1024)S(1)} %get-tuple-element.48, f32[768]{0:T(1024)S(1)} %get-tuple-element.47), channel_id=1, replica_groups=mesh['kv'=8,'z'=8,'y'=4] {'kv','y'}, use_global_device_ids=true, to_apply=%region_10.11 | all-reduce | flops 2304 | bytes 18432 | tf_op jit(solution)/shard_map/psum | solution.py:153
  (54 shorter events, 6.4 us)
Async XLA Ops:
  8.0 107.9 %copy-start = (bf16[256,2048]{1,0:T(8,128)(2,1)S(1)}, bf16[256,2048]{1,0:T(8,128)(2,1)}, u32[]{:S(2)}) copy-start(bf16[256,2048]{1,0:T(8,128)(2,1)} %param.18) | copy-start | bytes 3145732
  8.0 10.3 %copy-start.1 = (bf16[192,2048]{1,0:T(8,128)(2,1)S(1)}, bf16[192,2048]{1,0:T(8,128)(2,1)}, u32[]{:S(2)}) copy-start(bf16[192,2048]{1,0:T(8,128)(2,1)} %param.13) | copy-start | bytes 2359300
  8.0 10.3 %copy-start.5 = (f32[2048]{0:T(1024)S(1)}, f32[2048]{0:T(1024)}, u32[]{:S(2)}) copy-start(f32[2048]{0:T(1024)} %param.14) | copy-start | bytes 24580
  8.0 10.3 %copy-start.4 = (bf16[2048,256]{1,0:T(8,128)(2,1)S(1)}, bf16[2048,256]{1,0:T(8,128)(2,1)}, u32[]{:S(2)}) copy-start(bf16[2048,256]{1,0:T(8,128)(2,1)} %param.15) | copy-start | bytes 3145732
  8.0 86.5 %all-gather.5.cloned.1.call-start = ((), (), s32[]{:S(2)}) async-start(), calls=%async_computation | async-start | bytes 1622016 | tf_op jit(solution)/shard_map/all_gather | solution.py:87
  15.6 170.5 %all-reduce.4.cloned.1.call-start = ((), (), s32[]{:S(2)}) async-start(), calls=%async_computation.1 | async-start | bytes 3145728 | tf_op jit(solution)/shard_map/psum | solution.py:130
  115.9 72.0 %copy-start.2 = (f32[2048]{0:T(1024)S(1)}, f32[2048]{0:T(1024)}, u32[]{:S(2)}) copy-start(f32[2048]{0:T(1024)} %param.19) | copy-start | bytes 24580
  117.6 73.1 %copy-start.6 = (u32[256]{0:T(256)S(1)}, u32[256]{0:T(256)}, u32[]{:S(2)}) copy-start(u32[256]{0:T(256)} %constant.73) | copy-start | bytes 3076
  117.6 75.1 %copy-start.3 = (s32[193]{0:T(256)S(1)}, s32[193]{0:T(256)}, u32[]{:S(2)}) copy-start(s32[193]{0:T(256)} %param.23) | copy-start | bytes 2320
  117.6 89.4 %all-gather.9.cloned.1.call-start = ((), (), s32[]{:S(2)}) async-start(), calls=%async_computation.3 | async-start | bytes 7372800 | tf_op jit(solution)/shard_map/all_gather | solution.py:134
  118.2 119.0 %all-gather.7.cloned.1.call-start = ((), (), s32[]{:S(2)}) async-start(), calls=%async_computation.2 | async-start | bytes 3932160 | tf_op jit(solution)/shard_map/all_gather | solution.py:132
Sparse Core Ops, SparseCore 0:
  15.7 78.7 all-gather.4
  117.7 68.2 all-reduce.3
Sparse Core Ops, SparseCore 1:
  119.9 73.3 all-gather.8
  194.9 42.3 all-gather.6
where the time goes:
time: 450 us; the launch traced here: 449 us
  blocking collectives  203 us (45%)
  waiting for transfers between devices  166 us (37%)
  matrix products  26.6 us (6%)
  other arithmetic  19.3 us (4%)
  between operations  17.7 us (4%)
  local copies, waits for them, and re-layouts  16.2 us (4%)
    psum x1, blocking collectives, local(): lax.psum((row_stats[1] * rescale, rescale * (row_stats[2] + (row_stats[0]...  124 us
    all_gather x1, waiting for transfers between devices, local(): shard_rows = lax.all_gather(packed, ('z', 'y'), axis=0, tiled=True)  75.5 us
    psum x1, waiting for transfers between devices, local(): lax.psum(jnp.dot(context, w_o, preferred_element_type=jnp.float32), 'kv')  67.6 us
    pmax x1, blocking collectives, local(): top_all = lax.pmax(row_stats[0], ('kv', 'y'))  64.9 us
    all_gather x1, waiting for transfers between devices, local(): head_rows = lax.all_gather(final_in, 'y', axis=0, tiled=True)  22.4 us
    unnamed x1, blocking collectives  14 us
    dot_general x1, matrix products, local(): jnp.dot(head_rows, head_cols, preferred_element_type=jnp.float32)  9.77 us
  transfers between devices with their start and end apart: 4, of which 3 were waited for; matrix products, arithmetic and copies ran while one was open for 4% of the time, Pallas kernels for 0%

commit v1 on v0

--- a/solution.py
+++ b/solution.py
@@ -84,7 +84,8 @@
         jnp.zeros((kv_local, group_size, tok_rows), jnp.float32),
         jnp.zeros((kv_local, group_size, tok_rows, HEAD_DIM), jnp.float32),
     )
-    shard_rows = lax.all_gather(packed, ("z", "y"), axis=0, tiled=True)
+    sent = jnp.stack([packed] * lax.axis_size(("z", "y")))
+    shard_rows = jnp.concatenate(lax.all_to_all(sent, ("z", "y"), 0, 0), axis=0)
     offset = jnp.int32(0)
     row_count = shard_rows.shape[0]
     key_pos = jnp.arange(row_count, dtype=jnp.int32)

time: 450 us -> 428 us (0.951)
  waiting for transfers between devices: 166 us -> 123 us
  starting transfers between devices: 0.35 us -> 11.5 us
  matrix products: 26.6 us -> 35 us
    all_gather x1 -> x0, waiting for transfers between devices: 75.5 us -> none  [local(): shard_rows = lax.all_gather(packed, ('z', 'y'), axis=0, tiled=True)]
    all_to_all x0 -> x1, waiting for transfers between devices: none -> 33.2 us  [local(): shard_rows = jnp.concatenate(lax.all_to_all(sent, ('z', 'y'), 0, 0), axis=0)]
    all_to_all x0 -> x1, starting transfers between devices: none -> 11.4 us  [local(): shard_rows = jnp.concatenate(lax.all_to_all(sent, ('z', 'y'), 0, 0), axis=0)]
where the time goes in v1:
time: 428 us
  blocking collectives  203 us (47%)
  waiting for transfers between devices  123 us (29%)
  matrix products  35 us (8%)
  other arithmetic  23 us (5%)
  between operations  17.7 us (4%)
  local copies, waits for them, and re-layouts  14.4 us (3%)
  starting transfers between devices  11.5 us (3%)
    psum x1, blocking collectives, local(): lax.psum((row_stats[1] * rescale, rescale * (row_stats[2] + (row_stats[0]...  124 us
    psum x1, waiting for transfers between devices, local(): lax.psum(jnp.dot(context, w_o, preferred_element_type=jnp.float32), 'kv')  67.3 us
    pmax x1, blocking collectives, local(): top_all = lax.pmax(row_stats[0], ('kv', 'y'))  64.9 us
    all_to_all x1, waiting for transfers between devices, local(): shard_rows = jnp.concatenate(lax.all_to_all(sent, ('z', 'y'), 0, 0), axis=0)  33.2 us
    all_gather x1, waiting for transfers between devices, local(): head_rows = lax.all_gather(final_in, 'y', axis=0, tiled=True)  22.2 us
    unnamed x1, blocking collectives  14.2 us
    all_to_all x1, starting transfers between devices, local(): shard_rows = jnp.concatenate(lax.all_to_all(sent, ('z', 'y'), 0, 0), axis=0)  11.4 us
    dot_general x1, matrix products, local(): jnp.dot(head_rows, head_cols, preferred_element_type=jnp.float32)  9.79 us
  transfers between devices with their start and end apart: 4, of which 3 were waited for; matrix products, arithmetic and copies ran while one was open for 4% of the time, Pallas kernels for 0%

profile of v1, /device:TPU:32, one launch (start us, length us, event | category | flops | bytes accessed | tf_op | source)
XLA Modules:
  0.0 427.9 jit_solution(12811593413977909261)
XLA Ops:
  8.1 0.9 copy.28
  9.9 1.4 fusion.16
  11.3 1.6 convolution_bitcast_fusion
  12.9 1.6 convolution_convert_fusion
  14.9 1.5 stack.2
  16.4 11.4 %all-to-all-start = ((bf16[32,192,128]{2,1,0:T(8,128)(2,1)}), bf16[32,192,128]{2,1,0:T(8,128)(2,1)S(1)}, u32[]{:S(2)}, u32[]{:S(2)}) async-start(bf16[32,192,128]{2,1,0:T(8,128)(2,1)} %stack.2), calls=%async_computation | async-start | bytes 3145728 | tf_op jit(solution)/shard_map/all_to_all | solution.py:88
  30.4 1.8 fusion.31
  33.0 33.2 %all-to-all-done = bf16[32,192,128]{2,1,0:T(8,128)(2,1)S(1)} async-done(((bf16[32,192,128]{2,1,0:T(8,128)(2,1)}), bf16[32,192,128]{2,1,0:T(8,128)(2,1)S(1)}, u32[]{:S(2)}, u32[]{:S(2)}) %all-to-all-start) | async-done | bytes 1572896 | tf_op jit(solution)/shard_map/all_to_all | solution.py:88
  66.2 29.0 %conditional.1 = (f32[1,4,192]{2,1,0:T(4,128)S(1)}, f32[1,4,192,64]{2,3,1,0:T(8,128)S(1)}) conditional(s32[]{:T(128)} %bitcast.10, (s32[6144]{0:T(1024)S(1)}, s32[6144]{0:T(1024)S(1)}, s32[192]{0:T(256)S(1)}, s32[192]{0:T(256)S(1)}, bf16[32,192,128]{2,1,0:T(8,128)(2,1)S(1)}, /*index=5*/bf16[192,1,4,64]{0,3,2,1:T(8,128)(2,1)}) %tuple.16, () %tuple.17), branch_computations={%region_3.6_spmd, %region_6.7_spmd} | conditional | flops 1272839424 | bytes 64851472 | solution.py:118
  66.2 1.0 compare_and_fusion
  67.2 9.0 %fusion = (f32[4,192]{1,0:T(4,128)S(1)}, f32[6144,192,4]{0,1,2:T(8,128)}) fusion(pred[192,6144]{1,0:T(8,128)(4,1)S(1)} %compare_and_fusion, bf16[192,1,4,64]{0,3,2,1:T(8,128)(2,1)} %get-tuple-element.17, bf16[6144,128]{1,0:T(8,128)(2,1)S(1)} %bitcast.71), kind=kOutput, calls=%fused_computation.2 | convolution fusion | flops 618134784 | bytes 21728256 | tf_op jit(solution)/shard_map/cond/branch_0_fun/tkgd,skd->kgts/dot_general | solution.py:98
  76.2 9.4 %fusion.8 = f32[1,4,192,64]{2,3,1,0:T(8,128)S(1)} fusion(bf16[6144,128]{1,0:T(8,128)(2,1)S(1)} %bitcast.72, f32[6144,192,4]{0,1,2:T(8,128)} %get-tuple-element.31, f32[4,192]{1,0:T(4,128)S(1)} %broadcast_maximum_fusion, pred[192,6144]{1,0:T(8,128)(4,1)S(1)} %compare_and_fusion), kind=kOutput, calls=%fused_computation.12 | convolution fusion | flops 627572736 | bytes 21826560 | tf_op jit(solution)/shard_map/cond/branch_0_fun/kgts,skd->kgtd/dot_general | solution.py:109
  85.6 9.6 %fusion.2 = f32[4,192]{1,0:T(4,128)S(1)} fusion(f32[6144,192,4]{0,1,2:T(8,128)} %get-tuple-element.31, f32[4,192]{1,0:T(4,128)S(1)} %broadcast_maximum_fusion, pred[192,6144]{1,0:T(8,128)(4,1)S(1)} %compare_and_fusion), kind=kLoop, calls=%fused_computation.4 | loop fusion | flops 23592192 | bytes 20060160 | tf_op jit(solution)/shard_map/cond/branch_0_fun/reduce_sum | solution.py:108
  95.3 1.6 fusion.35
  97.6 67.3 %all-reduce.4.cloned.1.call-done = f32[192,2048]{1,0:T(8,128)} async-done(((f32[192,2048]{1,0:T(8,128)}), f32[192,2048]{1,0:T(8,128)}) %all-reduce.4.cloned.1.call-update) | async-done | bytes 1572880 | tf_op jit(solution)/shard_map/psum | solution.py:131
  164.9 1.7 multiply_reduce_fusion.1
  166.7 2.6 multiply_convert_fusion
  171.7 14.2 %all-reduce = s32[1544]{0:T(1024)S(1)} all-reduce(s32[1544]{0:T(1024)S(1)} %dynamic-update-slice), channel_id=1, replica_groups=mesh['kv'=8,'z'=8,'y'=4] {'z'}, use_global_device_ids=true, to_apply=%add | all-reduce | flops 1544 | bytes 12352
  186.0 7.8 %reshape.290 = bf16[1544,2048]{1,0:T(8,128)(2,1)} reshape(bf16[8,193,2048]{2,1,0:T(8,128)(2,1)} %all-gather.6.cloned.1.call-done) | data formatting | bytes 12648448
  193.8 22.2 %all-gather.4.cloned.1.call-done = bf16[768,2048]{1,0:T(8,128)(2,1)} async-done(((bf16[192,2048]{1,0:T(8,128)(2,1)}), bf16[768,2048]{1,0:T(8,128)(2,1)}) %all-gather.4.cloned.1.call-update) | async-done | bytes 3145744 | tf_op jit(solution)/shard_map/all_gather | solution.py:133
  216.1 9.8 %select_reduce_fusion.1 = (f32[768]{0:T(1024)S(1)}, f32[768,1544]{0,1:T(8,128)}) fusion(pred[1544]{0:T(1024)(128)(4,1)S(1)} %broadcast_compare_fusion, bf16[768,2048]{1,0:T(8,128)(2,1)} %all-gather.4.cloned.1.call-done, bf16[1544,2048]{1,0:T(8,128)(2,1)} %reshape.290), kind=kOutput, calls=%fused_computation.23 | convolution fusion | flops 4860560384 | bytes 14217736 | tf_op jit(solution)/shard_map/dot_general | solution.py:145
  225.9 64.9 %pmax.7 = f32[768]{0:T(1024)S(1)} all-reduce(f32[768]{0:T(1024)S(1)} %get-tuple-element.42), channel_id=1, replica_groups=mesh['kv'=8,'z'=8,'y'=4] {'kv','y'}, use_global_device_ids=true, to_apply=%region_12.13 | all-reduce | flops 768 | bytes 6144 | tf_op jit(solution)/shard_map/pmax | solution.py:152
  290.8 4.5 %multiply_reduce_fusion = (f32[768]{0:T(1024)S(1)}, f32[768]{0:T(1024)S(1)}, f32[768]{0:T(1024)S(1)}) fusion(f32[768,1544]{0,1:T(8,128)} %get-tuple-element.43, f32[768]{0:T(1024)S(1)} %get-tuple-element.42, pred[1544]{0:T(1024)(128)(4,1)S(1)} %broadcast_compare_fusion, s32[1544]{0:T(1024)S(1)} %add.107, s32[768]{0:T(1024)S(1)} %dynamic_slice.9), kind=kLoop, calls=%fused_computation.18 | loop fusion | flops 13041408 | bytes 4766248 | tf_op jit(solution)/shard_map/reduce_sum | solution.py:151
  295.3 123.8 %all-reduce.1 = (f32[768]{0:T(1024)S(1)}, f32[768]{0:T(1024)S(1)}, f32[768]{0:T(1024)S(1)}) all-reduce(f32[768]{0:T(1024)S(1)} %get-tuple-element.26, f32[768]{0:T(1024)S(1)} %get-tuple-element.37, f32[768]{0:T(1024)S(1)} %get-tuple-element.36), channel_id=1, replica_groups=mesh['kv'=8,'z'=8,'y'=4] {'kv','y'}, use_global_device_ids=true, to_apply=%region_10.11 | all-reduce | flops 2304 | bytes 18432 | tf_op jit(solution)/shard_map/psum | solution.py:154
  (51 shorter events, 7.1 us)
Async XLA Ops:
  8.0 87.3 %copy-start = (bf16[256,2048]{1,0:T(8,128)(2,1)S(1)}, bf16[256,2048]{1,0:T(8,128)(2,1)}, u32[]{:S(2)}) copy-start(bf16[256,2048]{1,0:T(8,128)(2,1)} %param.18) | copy-start | bytes 3145732
  8.0 22.4 %copy-start.1 = (bf16[192,2048]{1,0:T(8,128)(2,1)S(1)}, bf16[192,2048]{1,0:T(8,128)(2,1)}, u32[]{:S(2)}) copy-start(bf16[192,2048]{1,0:T(8,128)(2,1)} %param.13) | copy-start | bytes 2359300
  8.0 22.4 %copy-start.4 = (f32[2048]{0:T(1024)S(1)}, f32[2048]{0:T(1024)}, u32[]{:S(2)}) copy-start(f32[2048]{0:T(1024)} %param.14) | copy-start | bytes 24580
  16.4 49.8 %all-to-all-start = ((bf16[32,192,128]{2,1,0:T(8,128)(2,1)}), bf16[32,192,128]{2,1,0:T(8,128)(2,1)S(1)}, u32[]{:S(2)}, u32[]{:S(2)}) async-start(bf16[32,192,128]{2,1,0:T(8,128)(2,1)} %stack.2), calls=%async_computation | async-start | bytes 3145728 | tf_op jit(solution)/shard_map/all_to_all | solution.py:88
  27.8 137.1 %all-reduce.4.cloned.1.call-start = ((), (), s32[]{:S(2)}) async-start(), calls=%async_computation.1 | async-start | bytes 3145728 | tf_op jit(solution)/shard_map/psum | solution.py:131
  95.3 71.4 %copy-start.2 = (f32[2048]{0:T(1024)S(1)}, f32[2048]{0:T(1024)}, u32[]{:S(2)}) copy-start(f32[2048]{0:T(1024)} %param.19) | copy-start | bytes 24580
  97.0 72.5 %copy-start.5 = (u32[256]{0:T(256)S(1)}, u32[256]{0:T(256)}, u32[]{:S(2)}) copy-start(u32[256]{0:T(256)} %constant.73) | copy-start | bytes 3076
  97.0 74.5 %copy-start.3 = (s32[193]{0:T(256)S(1)}, s32[193]{0:T(256)}, u32[]{:S(2)}) copy-start(s32[193]{0:T(256)} %param.23) | copy-start | bytes 2320
  97.0 89.0 %all-gather.6.cloned.1.call-start = ((), (), s32[]{:S(2)}) async-start(), calls=%async_computation.3 | async-start | bytes 7372800 | tf_op jit(solution)/shard_map/all_gather | solution.py:135
  97.6 118.5 %all-gather.4.cloned.1.call-start = ((), (), s32[]{:S(2)}) async-start(), calls=%async_computation.2 | async-start | bytes 3932160 | tf_op jit(solution)/shard_map/all_gather | solution.py:133
Sparse Core Ops, SparseCore 0:
  97.1 67.7 all-reduce.3
Sparse Core Ops, SparseCore 1:
  99.3 72.8 all-gather.5
  173.8 42.2 all-gather.3
